TPU v7x, 32 devices: a whole 2x2x4 slice. The times are simulated.
32 devices in a mesh: tm: 16 (over z, x, core), doc: 2 (over y).
Axes of the slice: x: 2, y: 2, z: 4, core: 2. Of those that a mesh axis runs over, the one named last changes fastest.
Arguments:
- beta: float32 [16, 4096, 128], P('tm', 'doc'), may hold values from -6 to 260
- word_ids: int32 [16, 8, 128], P('tm', 'doc'), may hold values from 0 to 4095
- word_counts: int32 [16, 8, 128], P('tm', 'doc'), may hold values from 1 to 8
- block_slot: int32 [32], replicated, may hold values from 0 to 31, each once
- topic_prior: float32 [128], replicated, may hold values from 0.05 to 0.5
- drift_var: float32 [128], replicated, may hold values from 0.0005 to 0.05
- obs_precision: float32 [16, 128], replicated, may hold values from 0.01 to 4
Outputs:
- smoothed_means: float32 [16, 4096, 128], P('tm', 'doc')
- doc_topics: float32 [16, 8, 128], P('tm', 'doc')
Inputs may be any that keep to these rules, and one draw needn't show every extreme that they name: `block_slot`: each block has its own position.
All inputs are finite; a program needn't handle non-finite values.
Results may differ from a plain program's by a relative error of at most 0.0012.
The roundings to bfloat16 on the way count: a program that leaves them out, or rounds other values in their place, can miss the bound.
Values may be sent and summed in bfloat16 or wider, within the bound.
No kernel may reach another device: no remote copies, remote signals or barrier semaphores. Data moves between devices by JAX's collectives and lax.ppermute only.
A program may use at most 192 MiB of HBM per device.

v0:
```python
import jax
import jax.numpy as jnp
from jax import lax
from jax.sharding import PartitionSpec as P

K = 128
BLOCK = 128
EITERS = 4
init_variance = 4.0


def variance_tables(obs_precision, drift_var):

    def forward_step(prior_var, precision):
        denominator = 1.0 + prior_var * precision
        gain_now = prior_var * precision / denominator
        filt_var = prior_var / denominator
        return (filt_var + drift_var, (gain_now, filt_var))

    start_var = jnp.full(drift_var.shape, init_variance, dtype=jnp.float32)
    last_var, (gains, filt_vars) = lax.scan(forward_step, start_var, obs_precision)

    def backward_step(info_next, precision):
        merged = info_next + precision
        shrink = 1.0 / (1.0 + drift_var * merged)
        info_now = merged * shrink
        return (info_now, (shrink, info_now))

    zero_info = jnp.zeros(drift_var.shape, dtype=jnp.float32)
    last_info, (shrinks, infos) = lax.scan(
        backward_step, zero_info, obs_precision[1:], reverse=True
    )
    shrinks = jnp.concatenate([shrinks, jnp.ones_like(zero_info)[None]], axis=0)
    infos = jnp.concatenate([infos, zero_info[None]], axis=0)
    return (gains, filt_vars, shrinks, infos)


def e_step(looked, word_counts, topic_prior):
    counts_float = word_counts.astype(jnp.float32)
    doc_topics = topic_prior + jnp.sum(counts_float, axis=-1, keepdims=True) / K
    scores = looked.astype(jnp.float32)
    for sweep in range(EITERS):
        resp = jax.nn.softmax(lax.digamma(doc_topics)[..., None, :] + scores, axis=-1)
        doc_topics = topic_prior + jnp.sum(counts_float[..., None] * resp, axis=-2)
    weighted = (counts_float[..., None] * resp).astype(jnp.bfloat16)
    return (doc_topics, weighted)


def body(beta, word_ids, word_counts, block_slot, topic_prior, drift_var, obs_precision):
    local_beta = beta[0]
    own_words = local_beta.shape[0]
    topics = local_beta.shape[1]
    doc_devices = lax.axis_size("doc")
    doc_place = lax.axis_index("doc")
    local_peak = jnp.max(local_beta, axis=0)
    local_total = jnp.sum(jnp.exp(local_beta - local_peak), axis=0)
    slot_ids = word_ids[0]
    local_docs = slot_ids.shape[0]
    slot_width = slot_ids.shape[1]
    columns = jnp.take(block_slot, slot_ids // BLOCK) * BLOCK + slot_ids % BLOCK
    all_columns = lax.all_gather(columns, "doc", axis=0, tiled=True)
    all_counts = lax.all_gather(word_counts[0], "doc", axis=0, tiled=True)
    peaks = lax.all_gather(local_peak, "doc")
    totals = lax.all_gather(local_total, "doc")
    peak_value = jnp.max(peaks, axis=0)
    total_value = jnp.sum(totals * jnp.exp(peaks - peak_value), axis=0)
    normalizer = peak_value + jnp.log(total_value)
    flat_columns = all_columns.reshape(-1)
    local_columns = flat_columns - doc_place * own_words
    inside = (local_columns >= 0) & (local_columns < own_words)
    picked = jnp.take(local_beta, jnp.clip(local_columns, 0, own_words - 1), axis=0)
    partial = jnp.where(
        inside[:, None], (picked - normalizer).astype(jnp.bfloat16), jnp.zeros((), jnp.bfloat16)
    )
    looked = lax.psum(partial, "doc").reshape(local_docs * doc_devices, slot_width, topics)
    doc_topics_all, weighted = e_step(looked, all_counts, topic_prior)
    doc_topics = lax.dynamic_slice_in_dim(doc_topics_all, doc_place * local_docs, local_docs, 0)
    flat_weighted = weighted.reshape(-1, topics)
    row_words = lax.iota(jnp.int32, own_words)
    marks = (row_words[:, None] == local_columns[None, :]).astype(jnp.bfloat16)
    counts = jnp.dot(marks, flat_weighted, preferred_element_type=jnp.float32)
    pseudo = local_beta + jnp.log1p(counts)
    gains, filt_vars, shrinks, infos = variance_tables(obs_precision, drift_var)
    years_total = obs_precision.shape[0]
    pulls = filt_vars / (filt_vars + drift_var)
    pulls = pulls.at[-1].set(0.0)
    years = lax.axis_size("tm")
    chunk = own_words // years
    by_year = lax.all_to_all(
        pseudo.reshape(years, chunk, topics), "tm", split_axis=0, concat_axis=0, tiled=True
    )

    def filter_step(mean_prev, inputs):
        gain_now, pseudo_now = inputs
        mean_now = (1.0 - gain_now) * mean_prev + gain_now * pseudo_now
        return (mean_now, mean_now)

    zero_mean = jnp.zeros((chunk, topics), dtype=jnp.float32)
    last_mean, filtered = lax.scan(
        filter_step, zero_mean, (gains[:, None, :], by_year), unroll=True
    )

    def smooth_step(mean_next, inputs):
        pull_now, filt_now = inputs
        mean_now = pull_now * mean_next + (1.0 - pull_now) * filt_now
        return (mean_now, mean_now)

    first_mean, smoothed = lax.scan(
        smooth_step, zero_mean, (pulls[:, None, :], filtered), reverse=True, unroll=True
    )
    back = lax.all_to_all(smoothed, "tm", split_axis=0, concat_axis=0, tiled=True)
    return (back.reshape(own_words, topics)[None], doc_topics[None])


def solution(mesh):
    in_specs = (
        P("tm", "doc", None),
        P("tm", "doc", None),
        P("tm", "doc", None),
        P(),
        P(),
        P(),
        P(),
    )
    out_specs = (P("tm", "doc", None), P("tm", "doc", None))
    return jax.shard_map(body, mesh=mesh, in_specs=in_specs, out_specs=out_specs, check_vma=False)
```

profile of v0, /device:TPU:9, one launch (start us, length us, event | category | flops | bytes accessed | tf_op | source)
XLA Modules:
  0.0 144.6 jit_solution(16217126004983186146)
XLA Ops:
  7.2 1.6 %reduce_max.54 = f32[128]{0:T(128)S(1)} reduce(f32[1,2048,128]{2,1,0:T(8,128)} %param.11, f32[]{:T(128)} %constant.154.clone.1), dimensions={0,1}, to_apply=%region_3.4 | reduce | flops 262016 | bytes 1049092 | tf_op jit(solution)/shard_map/reduce_max | solution.py:55
  9.1 3.1 %all-gather.5 = f32[2,1,128]{2,1,0:T(1,128)S(1)} all-gather(f32[1,1,128]{2,1,0:T(1,128)S(1)} %bitcast.281), channel_id=4, replica_groups=mesh['tm'=16,'doc'=2] {'doc'}, dimensions={0}, use_global_device_ids=true | all-gather | bytes 1536 | tf_op jit(solution)/shard_map/all_gather | solution.py:64
  12.2 3.1 %all-gather.4 = f32[2,1,128]{2,1,0:T(1,128)S(1)} all-gather(f32[1,1,128]{2,1,0:T(1,128)S(1)} %bitcast.278), channel_id=3, replica_groups=mesh['tm'=16,'doc'=2] {'doc'}, dimensions={0}, use_global_device_ids=true | all-gather | bytes 1536 | tf_op jit(solution)/shard_map/all_gather | solution.py:63
  15.4 3.3 %gather_fusion = s32[512]{0:T(512)S(1)} fusion(s32[32]{0:T(128)S(1)} %copy-done, s32[1024]{0:T(1024)S(1)} %pad_clamp_fusion), kind=kCustom, calls=%fused_computation | custom fusion | bytes 6144 | tf_op jit(solution)/shard_map/jit(_take)/gather | solution.py:60
  18.8 3.2 %all-gather.3 = s32[2,4,128]{2,1,0:T(4,128)S(1)} all-gather(s32[1,4,128]{2,1,0:T(4,128)S(1)} %fusion.120), channel_id=1, replica_groups=mesh['tm'=16,'doc'=2] {'doc'}, dimensions={0}, use_global_device_ids=true | all-gather | bytes 6144 | tf_op jit(solution)/shard_map/all_gather | solution.py:61
  22.0 2.8 %gather_fusion.1 = f32[1024,128]{1,0:T(8,128)S(1)} fusion(f32[2048,128]{1,0:T(8,128)S(1)} %bitcast.257, s32[1024]{0:T(1024)S(1)} %broadcast_clamp_fusion), kind=kCustom, calls=%fused_computation.1 | custom fusion | bytes 1052672 | tf_op jit(solution)/shard_map/jit(_take)/gather | solution.py:71
  24.9 1.0 fusion.24
  25.9 3.2 %all-gather = s32[1,8,128]{2,0,1:T(1,128)S(1)} all-gather(s32[1,4,128]{2,0,1:T(1,128)S(1)} %bitcast.279), channel_id=2, replica_groups=mesh['tm'=16,'doc'=2] {'doc'}, dimensions={1}, use_global_device_ids=true | all-gather | bytes 6144 | tf_op jit(solution)/shard_map/all_gather | solution.py:62
  29.5 24.0 %all-reduce.2.cloned.1.call-done = bf16[1024,128]{1,0:T(8,128)(2,1)} async-done(((bf16[1024,128]{1,0:T(8,128)(2,1)}), bf16[1024,128]{1,0:T(8,128)(2,1)}) %all-reduce.2.cloned.1.call-update) | async-done | bytes 262160 | tf_op jit(solution)/shard_map/psum | solution.py:75
  53.5 1.2 fusion.6
  54.7 1.3 fusion.23
  56.1 1.4 multiply_reduce_fusion.3
  57.5 1.2 fusion.8
  61.9 2.8 %fusion.4 = f32[2048,128]{1,0:T(8,128)} fusion(bf16[1024,128]{1,0:T(8,128)(2,1)S(1)} %fusion.17, s32[1024]{0:T(1024)S(1)} %bitcast.274, f32[1,2048,128]{2,1,0:T(8,128)S(1)} %copy-done.2), kind=kOutput, calls=%fused_computation.11 | convolution fusion | flops 539230208 | bytes 2363392 | tf_op jit(solution)/shard_map/dot_general | solution.py:81
  64.7 7.0 %all-to-all-start = ((f32[16,128,128]{2,1,0:T(8,128)}), f32[16,128,128]{2,1,0:T(8,128)S(1)}, u32[]{:S(2)}, u32[]{:S(2)}) async-start(f32[16,128,128]{2,1,0:T(8,128)} %bitcast.59), calls=%async_computation | async-start | bytes 2097152 | tf_op jit(solution)/shard_map/all_to_all | solution.py:89
  71.7 12.5 %while.16 = (s32[]{:T(128)}, f32[128]{0:T(128)S(1)}, f32[16,128]{1,0:T(8,128)S(1)}, f32[16,128]{1,0:T(8,128)S(1)}, f32[16,128]{1,0:T(8,128)}, /*index=5*/f32[128]{0:T(128)S(1)}, s32[]{:T(128)}, s32[]{:T(128)}) while((s32[]{:T(128)}, f32[128]{0:T(128)S(1)}, f32[16,128]{1,0:T(8,128)S(1)}, f32[16,128]{1,0:T(8,128)S(1)}, ...), condition=%wide.region_1.0_spmd.clone, body=%wide.region_0.0_spmd.clone.sunk | while | flops 771 | bytes 5235 | solution.py:21
  71.7 0.7 fusion.137
  72.5 0.7 fusion.137
  73.3 0.7 fusion.137
  74.1 0.7 fusion.137
  74.8 0.7 fusion.137
  75.6 0.7 fusion.137
  76.4 0.7 fusion.137
  77.2 0.7 fusion.137
  78.0 0.7 fusion.137
  78.8 0.7 fusion.137
  79.5 0.7 fusion.137
  84.3 12.3 %all-to-all-done = f32[16,128,128]{2,1,0:T(8,128)S(1)} async-done(((f32[16,128,128]{2,1,0:T(8,128)}), f32[16,128,128]{2,1,0:T(8,128)S(1)}, u32[]{:S(2)}, u32[]{:S(2)}) %all-to-all-start) | async-done | bytes 1048608 | tf_op jit(solution)/shard_map/all_to_all | solution.py:89
  96.6 0.9 add_dynamic-update-slice_fusion
  107.1 4.8 %all-to-all-start.1 = ((f32[16,128,128]{2,1,0:T(8,128)}), f32[16,128,128]{2,1,0:T(8,128)S(1)}, u32[]{:S(2)}, u32[]{:S(2)}) async-start(f32[16,128,128]{2,1,0:T(8,128)} %fusion.41), calls=%async_computation.1 | async-start | bytes 2097152 | tf_op jit(solution)/shard_map/all_to_all | solution.py:111
  113.0 23.8 %all-to-all-done.1 = f32[16,128,128]{2,1,0:T(8,128)S(1)} async-done(((f32[16,128,128]{2,1,0:T(8,128)}), f32[16,128,128]{2,1,0:T(8,128)S(1)}, u32[]{:S(2)}, u32[]{:S(2)}) %all-to-all-start.1) | async-done | bytes 1048608 | tf_op jit(solution)/shard_map/all_to_all | solution.py:111
  136.8 1.0 copy.43
  (105 shorter events, 19.1 us)
Async XLA Ops:
  7.2 8.2 %copy-start = (s32[32]{0:T(128)S(1)}, s32[32]{0:T(128)}, u32[]{:S(2)}) copy-start(s32[32]{0:T(128)} %param.14) | copy-start | bytes 388
  7.2 1.7 %copy-start.2 = (f32[1,2048,128]{2,1,0:T(8,128)S(1)}, f32[1,2048,128]{2,1,0:T(8,128)}, u32[]{:S(2)}) copy-start(f32[1,2048,128]{2,1,0:T(8,128)} %param.11) | copy-start | bytes 3145732
  7.2 46.3 %all-reduce.2.cloned.1.call-start = ((), (), s32[]{:S(2)}) async-start(), calls=%async_computation.2 | async-start | bytes 524288 | tf_op jit(solution)/shard_map/psum | solution.py:75
  7.2 8.1 %copy-start.5 = (s32[1,4,128]{2,1,0:T(4,128)S(1)}, s32[1,4,128]{2,1,0:T(4,128)}, u32[]{:S(2)}) copy-start(s32[1,4,128]{2,1,0:T(4,128)} %param.12) | copy-start | bytes 6148
  24.8 1.1 copy-start.6
  24.8 4.5 %copy-start.4 = (f32[128]{0:T(128)S(1)}, f32[128]{0:T(128)}, u32[]{:S(2)}) copy-start(f32[128]{0:T(128)} %param.15) | copy-start | bytes 1540
  53.5 5.2 %copy-start.1 = (bf16[1024,128]{1,0:T(8,128)(2,1)S(1)}, bf16[1024,128]{1,0:T(8,128)(2,1)}, u32[]{:S(2)}) copy-start(bf16[1024,128]{1,0:T(8,128)(2,1)} %all-reduce.2.cloned.1.call-done) | copy-start | bytes 786436
  64.7 7.0 %copy-start.3 = (f32[128]{0:T(128)S(1)}, f32[128]{0:T(128)}, u32[]{:S(2)}) copy-start(f32[128]{0:T(128)} %param.16) | copy-start | bytes 1540
  64.7 31.9 %all-to-all-start = ((f32[16,128,128]{2,1,0:T(8,128)}), f32[16,128,128]{2,1,0:T(8,128)S(1)}, u32[]{:S(2)}, u32[]{:S(2)}) async-start(f32[16,128,128]{2,1,0:T(8,128)} %bitcast.59), calls=%async_computation | async-start | bytes 2097152 | tf_op jit(solution)/shard_map/all_to_all | solution.py:89
  107.1 29.7 %all-to-all-start.1 = ((f32[16,128,128]{2,1,0:T(8,128)}), f32[16,128,128]{2,1,0:T(8,128)S(1)}, u32[]{:S(2)}, u32[]{:S(2)}) async-start(f32[16,128,128]{2,1,0:T(8,128)} %fusion.41), calls=%async_computation.1 | async-start | bytes 2097152 | tf_op jit(solution)/shard_map/all_to_all | solution.py:111
Sparse Core Ops, SparseCore 0:
  26.0 27.4 all-reduce.1
where the time goes:
time: 146 us; the launch traced here: 145 us
  waiting for transfers between devices  60.2 us (41%)
  other arithmetic  29.6 us (20%)
  between operations  14.3 us (10%)
  local copies, waits for them, and re-layouts  13.1 us (9%)
  blocking collectives  12.6 us (9%)
  starting transfers between devices  11.8 us (8%)
  matrix products  2.76 us (2%)
    psum x1, waiting for transfers between devices, body(): lax.psum(partial, 'doc')  24 us
    all_to_all x1, waiting for transfers between devices, body(): lax.all_to_all(smoothed, 'tm', split_axis=0, concat_axis=0, tiled=True)  23.8 us
    all_to_all x1, waiting for transfers between devices, body(): lax.all_to_all(pseudo.reshape(years, chunk, topics), 'tm', split_axis=0,...  12.3 us
    add x16, other arithmetic, forward_step(): return (filt_var + drift_var, (gain_now, filt_var))  11.4 us
    all_to_all x1, starting transfers between devices, body(): lax.all_to_all(pseudo.reshape(years, chunk, topics), 'tm', split_axis=0,...  6.99 us
    unnamed x22, local copies, waits for them, and re-layouts  5.44 us
    unnamed x10, other arithmetic  5.43 us
    all_to_all x1, starting transfers between devices, body(): lax.all_to_all(smoothed, 'tm', split_axis=0, concat_axis=0, tiled=True)  4.76 us
  transfers between devices with their start and end apart: 3, of which 3 were waited for; matrix products, arithmetic and copies ran while one was open for 9% of the time, Pallas kernels for 0%

commit v1 on v0

--- a/solution.py
+++ b/solution.py
@@ -72,7 +72,9 @@
     partial = jnp.where(
         inside[:, None], (picked - normalizer).astype(jnp.bfloat16), jnp.zeros((), jnp.bfloat16)
     )
-    looked = lax.psum(partial, "doc").reshape(local_docs * doc_devices, slot_width, topics)
+    looked = jnp.sum(lax.all_gather(partial, "doc"), axis=0).reshape(
+        local_docs * doc_devices, slot_width, topics
+    )
     doc_topics_all, weighted = e_step(looked, all_counts, topic_prior)
     doc_topics = lax.dynamic_slice_in_dim(doc_topics_all, doc_place * local_docs, local_docs, 0)
     flat_weighted = weighted.reshape(-1, topics)

time: 146 us -> 118 us (0.81)
  waiting for transfers between devices: 60.2 us -> 36.1 us
  between operations: 14.3 us -> 0.92 us
  blocking collectives: 12.6 us -> 18.7 us
  starting transfers between devices: 11.8 us -> 17.2 us
  other arithmetic: 29.6 us -> 27.8 us
    psum x1 -> x0, waiting for transfers between devices: 24 us -> none  [body(): lax.psum(partial, 'doc')]
    all_gather x0 -> x1, blocking collectives: none -> 5.89 us  [body(): lax.all_gather(partial, 'doc')]
    div x0 -> x3, other arithmetic: none -> 5.83 us  [e_step(): jax.nn.softmax(lax.digamma(doc_topics)[..., None, :] + scores, axis=-1)]
    all_to_all x1, starting transfers between devices: 6.99 us -> 12.4 us  [body(): lax.all_to_all(pseudo.reshape(years, chunk, topics), 'tm', split_axis=0,...]
    reduce_max x4 -> x1, other arithmetic: 2.83 us -> 0.22 us  [e_step(): jax.nn.softmax(lax.digamma(doc_topics)[..., None, :] + scores, axis=-1)]
    reduce_sum x4 -> x1, other arithmetic: 2.88 us -> 0.48 us  [e_step(): doc_topics = topic_prior + jnp.sum(counts_float[..., None] * resp, axis=-2)]
    reduce_sum x4 -> x1, other arithmetic: 2.48 us -> 0.39 us  [e_step(): jax.nn.softmax(lax.digamma(doc_topics)[..., None, :] + scores, axis=-1)]
    unnamed x22 -> x18, local copies, waits for them, and re-layouts: 5.44 us -> 5.44 us
  transfers between devices with their start and end apart: 3 -> 2, of which waited for: 3 -> 2; matrix products, arithmetic and copies ran while one was open for 9% -> 11% of each run, Pallas kernels for 0% -> 0%
where the time goes in v1:
time: 118 us; the launch traced here: 117 us
  waiting for transfers between devices  36.1 us (31%)
  other arithmetic  27.8 us (24%)
  blocking collectives  18.7 us (16%)
  starting transfers between devices  17.2 us (15%)
  local copies, waits for them, and re-layouts  13.1 us (11%)
  matrix products  2.76 us (2%)
    all_to_all x1, waiting for transfers between devices, body(): lax.all_to_all(smoothed, 'tm', split_axis=0, concat_axis=0, tiled=True)  23.8 us
    all_to_all x1, starting transfers between devices, body(): lax.all_to_all(pseudo.reshape(years, chunk, topics), 'tm', split_axis=0,...  12.4 us
    all_to_all x1, waiting for transfers between devices, body(): lax.all_to_all(pseudo.reshape(years, chunk, topics), 'tm', split_axis=0,...  12.3 us
    add x16, other arithmetic, forward_step(): return (filt_var + drift_var, (gain_now, filt_var))  11.3 us
    all_gather x1, blocking collectives, body(): lax.all_gather(partial, 'doc')  5.89 us
    div x3, other arithmetic, e_step(): jax.nn.softmax(lax.digamma(doc_topics)[..., None, :] + scores, axis=-1)  5.83 us
    unnamed x18, local copies, waits for them, and re-layouts  5.44 us
    unnamed x10, other arithmetic  5.43 us
  transfers between devices with their start and end apart: 2, of which 2 were waited for; matrix products, arithmetic and copies ran while one was open for 11% of the time, Pallas kernels for 0%

profile of v1, /device:TPU:9, one launch (start us, length us, event | category | flops | bytes accessed | tf_op | source)
XLA Modules:
  0.0 116.9 jit_solution(3678050226903893093)
XLA Ops:
  0.7 3.5 %all-gather = s32[1,8,128]{2,0,1:T(1,128)S(1)} all-gather(s32[1,4,128]{2,0,1:T(1,128)} %bitcast.243), channel_id=2, replica_groups=mesh['tm'=16,'doc'=2] {'doc'}, dimensions={1}, use_global_device_ids=true | all-gather | bytes 6144 | tf_op jit(solution)/shard_map/all_gather | solution.py:62
  4.3 1.5 %reduce_max.56 = f32[128]{0:T(128)S(1)} reduce(f32[1,2048,128]{2,1,0:T(8,128)} %param.11, f32[]{:T(128)} %constant.155.clone.1), dimensions={0,1}, to_apply=%region_3.4 | reduce | flops 262016 | bytes 1049092 | tf_op jit(solution)/shard_map/reduce_max | solution.py:55
  6.1 3.1 %all-gather.5 = f32[2,1,128]{2,1,0:T(1,128)S(1)} all-gather(f32[1,1,128]{2,1,0:T(1,128)S(1)} %bitcast.245), channel_id=4, replica_groups=mesh['tm'=16,'doc'=2] {'doc'}, dimensions={0}, use_global_device_ids=true | all-gather | bytes 1536 | tf_op jit(solution)/shard_map/all_gather | solution.py:64
  9.2 3.1 %all-gather.4 = f32[2,1,128]{2,1,0:T(1,128)S(1)} all-gather(f32[1,1,128]{2,1,0:T(1,128)S(1)} %bitcast.242), channel_id=3, replica_groups=mesh['tm'=16,'doc'=2] {'doc'}, dimensions={0}, use_global_device_ids=true | all-gather | bytes 1536 | tf_op jit(solution)/shard_map/all_gather | solution.py:63
  12.4 3.3 %gather_fusion = s32[512]{0:T(512)S(1)} fusion(s32[32]{0:T(128)S(1)} %copy-done, s32[1024]{0:T(1024)S(1)} %pad_clamp_fusion), kind=kCustom, calls=%fused_computation | custom fusion | bytes 6144 | tf_op jit(solution)/shard_map/jit(_take)/gather | solution.py:60
  15.7 3.2 %all-gather.3 = s32[2,4,128]{2,1,0:T(4,128)S(1)} all-gather(s32[1,4,128]{2,1,0:T(4,128)S(1)} %fusion.139), channel_id=1, replica_groups=mesh['tm'=16,'doc'=2] {'doc'}, dimensions={0}, use_global_device_ids=true | all-gather | bytes 6144 | tf_op jit(solution)/shard_map/all_gather | solution.py:61
  19.0 2.8 %gather_fusion.1 = f32[1024,128]{1,0:T(8,128)S(1)} fusion(f32[2048,128]{1,0:T(8,128)S(1)} %bitcast.222, s32[1024]{0:T(1024)S(1)} %broadcast_clamp_fusion), kind=kCustom, calls=%fused_computation.1 | custom fusion | bytes 1052672 | tf_op jit(solution)/shard_map/jit(_take)/gather | solution.py:71
  22.2 5.9 %all_gather.28 = bf16[2,1024,128]{2,1,0:T(8,128)(2,1)S(1)} all-gather(bf16[1,1024,128]{2,1,0:T(8,128)(2,1)S(1)} %fusion.34), channel_id=1, replica_groups=mesh['tm'=16,'doc'=2] {'doc'}, dimensions={0}, use_global_device_ids=true | all-gather | bytes 786432 | tf_op jit(solution)/shard_map/all_gather | solution.py:75
  28.5 1.9 %fusion.157 = f32[8,128]{1,0:T(8,128)S(1)} fusion(f32[8,128,128]{2,1,0:T(8,128)S(1)} %bitcast.223, f32[8,128]{1,0:T(8,128)S(1)} %fusion.63, f32[8,128]{1,0:T(8,128)S(1)} %bitcast.232), kind=kOutput, calls=%fused_computation.314 | output fusion | flops 656638 | bytes 536576 | tf_op jit(solution)/shard_map/div | solution.py:43
  30.5 1.9 %fusion.160 = f32[8,128]{1,0:T(8,128)S(1)} fusion(f32[8,128,128]{2,1,0:T(8,128)S(1)} %bitcast.224, f32[8,128]{1,0:T(8,128)S(1)} %fusion.65, f32[8,128]{1,0:T(8,128)S(1)} %bitcast.233), kind=kOutput, calls=%fused_computation.315 | output fusion | flops 656638 | bytes 536576 | tf_op jit(solution)/shard_map/div | solution.py:43
  32.5 1.9 %fusion.163 = f32[8,128]{1,0:T(8,128)S(1)} fusion(f32[8,128,128]{2,1,0:T(8,128)S(1)} %bitcast.225, f32[8,128]{1,0:T(8,128)S(1)} %fusion.67, f32[8,128]{1,0:T(8,128)S(1)} %bitcast.234), kind=kOutput, calls=%fused_computation.316 | output fusion | flops 656638 | bytes 536576 | tf_op jit(solution)/shard_map/div | solution.py:43
  35.6 2.8 %fusion.10 = f32[2048,128]{1,0:T(8,128)} fusion(bf16[1024,128]{1,0:T(8,128)(2,1)S(1)} %fusion.29, s32[1024]{0:T(1024)S(1)} %bitcast.238, f32[1,2048,128]{2,1,0:T(8,128)S(1)} %copy-done.1), kind=kOutput, calls=%fused_computation.17 | convolution fusion | flops 539230208 | bytes 2363392 | tf_op jit(solution)/shard_map/dot_general | solution.py:83
  38.3 12.4 %all-to-all-start = ((f32[16,128,128]{2,1,0:T(8,128)}), f32[16,128,128]{2,1,0:T(8,128)S(1)}, u32[]{:S(2)}, u32[]{:S(2)}) async-start(f32[16,128,128]{2,1,0:T(8,128)} %bitcast.53), calls=%async_computation | async-start | bytes 2097152 | tf_op jit(solution)/shard_map/all_to_all | solution.py:91
  50.8 12.5 %while.16 = (s32[]{:T(128)}, f32[128]{0:T(128)S(1)}, f32[16,128]{1,0:T(8,128)S(1)}, f32[16,128]{1,0:T(8,128)S(1)}, f32[16,128]{1,0:T(8,128)}, /*index=5*/f32[128]{0:T(128)S(1)}, s32[]{:T(128)}, s32[]{:T(128)}) while((s32[]{:T(128)}, f32[128]{0:T(128)S(1)}, f32[16,128]{1,0:T(8,128)S(1)}, f32[16,128]{1,0:T(8,128)S(1)}, ...), condition=%wide.region_1.0_spmd.clone, body=%wide.region_0.0_spmd.clone.sunk | while | flops 771 | bytes 5235 | solution.py:21
  50.8 0.7 fusion.168
  51.6 0.7 fusion.168
  52.4 0.7 fusion.168
  53.2 0.7 fusion.168
  54.0 0.7 fusion.168
  54.7 0.7 fusion.168
  56.3 0.7 fusion.168
  57.1 0.7 fusion.168
  58.6 0.7 fusion.168
  59.4 0.7 fusion.168
  61.0 0.7 fusion.168
  61.8 0.7 fusion.168
  62.6 0.7 fusion.168
  63.4 12.3 %all-to-all-done = f32[16,128,128]{2,1,0:T(8,128)S(1)} async-done(((f32[16,128,128]{2,1,0:T(8,128)}), f32[16,128,128]{2,1,0:T(8,128)S(1)}, u32[]{:S(2)}, u32[]{:S(2)}) %all-to-all-start) | async-done | bytes 1048608 | tf_op jit(solution)/shard_map/all_to_all | solution.py:91
  75.7 0.9 add_dynamic-update-slice_fusion
  86.2 4.8 %all-to-all-start.1 = ((f32[16,128,128]{2,1,0:T(8,128)}), f32[16,128,128]{2,1,0:T(8,128)S(1)}, u32[]{:S(2)}, u32[]{:S(2)}) async-start(f32[16,128,128]{2,1,0:T(8,128)} %fusion.60), calls=%async_computation.1 | async-start | bytes 2097152 | tf_op jit(solution)/shard_map/all_to_all | solution.py:113
  92.1 23.8 %all-to-all-done.1 = f32[16,128,128]{2,1,0:T(8,128)S(1)} async-done(((f32[16,128,128]{2,1,0:T(8,128)}), f32[16,128,128]{2,1,0:T(8,128)S(1)}, u32[]{:S(2)}, u32[]{:S(2)}) %all-to-all-start.1) | async-done | bytes 1048608 | tf_op jit(solution)/shard_map/all_to_all | solution.py:113
  115.9 1.0 copy.43
  (95 shorter events, 16.2 us)
Async XLA Ops:
  0.6 11.7 %copy-start = (s32[32]{0:T(128)S(1)}, s32[32]{0:T(128)}, u32[]{:S(2)}) copy-start(s32[32]{0:T(128)} %param.14) | copy-start | bytes 388
  0.6 5.2 %copy-start.1 = (f32[1,2048,128]{2,1,0:T(8,128)S(1)}, f32[1,2048,128]{2,1,0:T(8,128)}, u32[]{:S(2)}) copy-start(f32[1,2048,128]{2,1,0:T(8,128)} %param.11) | copy-start | bytes 3145732
  4.3 8.0 %copy-start.4 = (s32[1,4,128]{2,1,0:T(4,128)S(1)}, s32[1,4,128]{2,1,0:T(4,128)}, u32[]{:S(2)}) copy-start(s32[1,4,128]{2,1,0:T(4,128)} %param.12) | copy-start | bytes 6148
  22.2 6.1 %copy-start.3 = (f32[128]{0:T(128)S(1)}, f32[128]{0:T(128)}, u32[]{:S(2)}) copy-start(f32[128]{0:T(128)} %param.15) | copy-start | bytes 1540
  38.3 12.5 %copy-start.2 = (f32[128]{0:T(128)S(1)}, f32[128]{0:T(128)}, u32[]{:S(2)}) copy-start(f32[128]{0:T(128)} %param.16) | copy-start | bytes 1540
  38.3 37.4 %all-to-all-start = ((f32[16,128,128]{2,1,0:T(8,128)}), f32[16,128,128]{2,1,0:T(8,128)S(1)}, u32[]{:S(2)}, u32[]{:S(2)}) async-start(f32[16,128,128]{2,1,0:T(8,128)} %bitcast.53), calls=%async_computation | async-start | bytes 2097152 | tf_op jit(solution)/shard_map/all_to_all | solution.py:91
  86.2 29.7 %all-to-all-start.1 = ((f32[16,128,128]{2,1,0:T(8,128)}), f32[16,128,128]{2,1,0:T(8,128)S(1)}, u32[]{:S(2)}, u32[]{:S(2)}) async-start(f32[16,128,128]{2,1,0:T(8,128)} %fusion.60), calls=%async_computation.1 | async-start | bytes 2097152 | tf_op jit(solution)/shard_map/all_to_all | solution.py:113
